TPU v7x, 32 devices: a whole 2x2x4 slice. The times are simulated.
32 devices in a mesh: seq: 8 (over y, x, core), head: 4 (over z).
Axes of the slice: x: 2, y: 2, z: 4, core: 2. Of those that a mesh axis runs over, the one named last changes fastest.
Arguments:
- queries: bfloat16 [2048, 4096], P('seq', 'head'), may hold values from -24 to 24
- keys: bfloat16 [2048, 4096], P('seq', 'head'), may hold values from -24 to 24
- values: bfloat16 [2048, 4096], P('seq', 'head'), may hold values from -6 to 6
- out_weight: bfloat16 [4096, 4096], P('head'), may hold values from -0.75 to 0.75
- global_blocks: int32 [2], replicated, may hold values from 0 to 31, as said below
- random_blocks: int32 [32, 3], replicated, may hold values from 0 to 31, as said below
- window_blocks: int32 [32], P('head'), may hold values from 1 to 2, as said below
- yarn_scale: int32 [1], replicated, may hold values from 2 to 64
- yarn_context: int32 [1], replicated, may hold values from 1024 to 4096
Outputs:
- mixed: bfloat16 [2048, 4096], P('seq', 'head')
Inputs may be any that keep to these rules, and one draw needn't show every extreme that they name: `global_blocks`: 2 different block numbers. `random_blocks`: of the 12 random blocks named by the query blocks of one index of seq, at most 2 lie among the blocks of any one index of seq, and some index of seq holds exactly 2 of them. `window_blocks`: some head has reach 2.
All inputs are finite; a program needn't handle non-finite values.
Results may differ from a plain program's by a relative error of at most 0.013.
Values may be sent and summed in bfloat16 or wider, within the bound.
No kernel may reach another device: no remote copies, remote signals or barrier semaphores. Data moves between devices by JAX's collectives and lax.ppermute only.
A program may use at most 128 MiB of HBM per device.

v0:
```python
import math
import jax
import jax.numpy as jnp
from jax import lax
from jax.sharding import PartitionSpec as P

HEAD_DIM = 128
BLOCK = 64
GLOB = 2
RAND = 3
WMAX = 2
masked_score = -1e30


def padded_2(cells, sides, width):
    for axis, dim in sides:
        count = lax.axis_size(axis)
        ends = count - 1
        head = lax.slice_in_dim(cells, 0, width, axis=dim)
        tail = lax.slice_in_dim(cells, cells.shape[dim] - width, cells.shape[dim], axis=dim)
        cells = jnp.concatenate(
            [
                lax.ppermute(tail, axis, [(i, (i + 1) % count) for i in range(ends)]),
                cells,
                lax.ppermute(head, axis, [((i + 1) % count, i) for i in range(ends)]),
            ],
            axis=dim,
        )
    return cells


def yarn_tables(yarn_scale, yarn_context):
    half_dim = HEAD_DIM // 2
    pair_index = jnp.arange(half_dim).astype(jnp.float32)
    base_rate = 10000.0 ** (-2.0 * pair_index / HEAD_DIM)
    factor = yarn_scale[0].astype(jnp.float32)
    context = yarn_context[0].astype(jnp.float32)
    turn_ratio = context * base_rate / (2.0 * math.pi)
    ramp_weight = jnp.clip((turn_ratio - 1.0) / 31.0, 0.0, 1.0)
    frequency = base_rate * ((1.0 - ramp_weight) / factor + ramp_weight)
    mscale = 0.1 * jnp.log(factor) + 1.0
    return (frequency, mscale)


def rotate(source, first_row, frequency, mscale):
    row_count, row_width = source.shape
    half_dim = HEAD_DIM // 2
    position = (first_row + jnp.arange(row_count)).astype(jnp.float32)
    angle_table = position[:, None] * frequency[None, :]
    cosine = jnp.cos(angle_table)[:, None, :] * mscale
    sine_part = jnp.sin(angle_table)[:, None, :] * mscale
    halves_view = source.astype(jnp.float32).reshape(row_count, row_width // HEAD_DIM, 2, half_dim)
    lower_half = halves_view[:, :, 0]
    upper_half = halves_view[:, :, 1]
    turned = jnp.stack(
        [
            lower_half * cosine - upper_half * sine_part,
            upper_half * cosine + lower_half * sine_part,
        ],
        axis=2,
    )
    return turned.reshape(row_count, row_width).astype(jnp.bfloat16)


def block_attend(query_blocks, key_blocks, value_blocks, valid_slots):
    count_q, slot_count = (key_blocks.shape[0], key_blocks.shape[1])
    heads_here = query_blocks.shape[-1] // HEAD_DIM
    query_grid = query_blocks.reshape(count_q, BLOCK, heads_here, HEAD_DIM)
    key_grid = key_blocks.reshape(count_q, slot_count * BLOCK, heads_here, HEAD_DIM)
    value_grid = value_blocks.reshape(count_q, slot_count * BLOCK, heads_here, HEAD_DIM)
    scores = jnp.einsum(
        "bqhd,bshd->bhqs", query_grid, key_grid, preferred_element_type=jnp.float32
    ) * (1.0 / math.sqrt(HEAD_DIM))
    present = jnp.repeat(jnp.transpose(valid_slots, (0, 2, 1)), BLOCK, axis=2)[:, :, None, :]
    scores = jnp.where(present, scores, masked_score)
    peak = jnp.max(scores, axis=3, keepdims=True)
    expo = jnp.exp(scores - peak)
    total = jnp.sum(expo, axis=3)
    weights = expo.astype(jnp.bfloat16)
    mixture = jnp.einsum("bhqs,bshd->bqhd", weights, value_grid, preferred_element_type=jnp.float32)
    mixture = mixture / jnp.transpose(total, (0, 2, 1))[..., None]
    return mixture.reshape(count_q, BLOCK, heads_here * HEAD_DIM).astype(jnp.bfloat16)


def on_device(
    queries,
    keys,
    values,
    out_weight,
    global_blocks,
    random_blocks,
    window_blocks,
    yarn_scale,
    yarn_context,
):
    tok_here, width_here = queries.shape
    heads_here = width_here // HEAD_DIM
    blocks_here = tok_here // BLOCK
    seq_count = lax.axis_size("seq")
    seq_place = lax.axis_index("seq")
    block_total = seq_count * blocks_here
    frequency, mscale = yarn_tables(yarn_scale, yarn_context)
    first_row = seq_place * tok_here
    query_rot = rotate(queries, first_row, frequency, mscale)
    key_rot = rotate(keys, first_row, frequency, mscale)
    pair_kv = jnp.stack([key_rot, values])
    padded = padded_2(pair_kv, (("seq", 1),), WMAX * BLOCK)
    padded_blocks = padded.reshape(2, blocks_here + 2 * WMAX, BLOCK, width_here)
    offsets = jnp.arange(-WMAX, WMAX + 1)
    window_ids = seq_place * blocks_here + jnp.arange(blocks_here)[:, None] + offsets[None, :]
    inside = (window_ids >= 0) & (window_ids < block_total)
    reach = jnp.abs(offsets)[None, :, None] <= window_blocks[None, None, :]
    window_valid = inside[:, :, None] & reach
    owner_global = global_blocks // blocks_here
    local_global = jnp.clip(global_blocks - seq_place * blocks_here, 0, blocks_here - 1)
    mine_global = owner_global == seq_place
    query_view = query_rot.reshape(blocks_here, BLOCK, width_here)
    key_view = key_rot.reshape(blocks_here, BLOCK, width_here)
    value_view = values.reshape(blocks_here, BLOCK, width_here)
    picked = jnp.stack([query_view[local_global], key_view[local_global], value_view[local_global]])
    masked = jnp.where(mine_global[None, :, None, None], picked.astype(jnp.float32), 0.0)
    shared = lax.psum(masked.astype(jnp.bfloat16), "seq")
    slot_total = blocks_here * RAND
    capacity = (slot_total + seq_count - 1) // seq_count
    flat_ids = random_blocks.reshape(seq_count, slot_total)
    owners = flat_ids // blocks_here
    slot_order = jnp.arange(slot_total)
    same_owner = (owners[:, :, None] == owners[:, None, :]) & (
        slot_order[None, None, :] < slot_order[None, :, None]
    )
    ranks = jnp.sum(same_owner.astype(jnp.int32), axis=2)
    local_ids = flat_ids - owners * blocks_here
    wanted = (owners[:, None, :] == seq_place) & (
        ranks[:, None, :] == jnp.arange(capacity)[None, :, None]
    )
    send_local = jnp.sum(jnp.where(wanted, local_ids[:, None, :], 0), axis=2)
    kv_blocks = pair_kv.reshape(2, blocks_here, BLOCK, width_here)
    outgoing = kv_blocks[:, send_local]
    incoming = lax.all_to_all(outgoing, "seq", split_axis=1, concat_axis=1, tiled=True)
    my_owners = owners[seq_place]
    my_ranks = ranks[seq_place]
    random_kv = incoming[:, my_owners, my_ranks].reshape(2, blocks_here, RAND, BLOCK, width_here)
    slot_parts = [
        padded_blocks[:, offset_slot : offset_slot + blocks_here][:, :, None]
        for offset_slot in range(2 * WMAX + 1)
    ]
    slot_parts.append(
        jnp.broadcast_to(shared[1:3][:, None], (2, blocks_here, GLOB, BLOCK, width_here))
    )
    slot_parts.append(random_kv)
    all_kv = jnp.concatenate(slot_parts, axis=2)
    all_valid = jnp.concatenate(
        [window_valid, jnp.ones((blocks_here, GLOB + RAND, heads_here), dtype=bool)], axis=1
    )
    attended = block_attend(query_view, all_kv[0], all_kv[1], all_valid)
    global_query = shared[0].reshape(GLOB, BLOCK, heads_here, HEAD_DIM)
    key_grid = key_rot.reshape(tok_here, heads_here, HEAD_DIM)
    value_grid = values.reshape(tok_here, heads_here, HEAD_DIM)
    global_scores = jnp.einsum(
        "gqhd,khd->ghqk", global_query, key_grid, preferred_element_type=jnp.float32
    ) * (1.0 / math.sqrt(HEAD_DIM))
    local_peak = jnp.max(global_scores, axis=3)
    peak = lax.pmax(local_peak, "seq")
    expo = jnp.exp(global_scores - peak[..., None])
    partial_total = jnp.sum(expo, axis=3)
    partial_mix = jnp.einsum(
        "ghqk,khd->gqhd", expo.astype(jnp.bfloat16), value_grid, preferred_element_type=jnp.float32
    )
    mix_sum, total_sum = (
        lax.psum(partial_mix.astype(jnp.bfloat16), "seq").astype(jnp.float32),
        lax.psum(partial_total.astype(jnp.bfloat16), "seq").astype(jnp.float32),
    )
    global_out = (
        (mix_sum / jnp.transpose(total_sum, (0, 2, 1))[..., None])
        .reshape(GLOB, BLOCK, width_here)
        .astype(jnp.bfloat16)
    )
    block_index = jnp.arange(blocks_here)
    for global_slot in range(GLOB):
        hit = mine_global[global_slot] & (block_index == local_global[global_slot])
        attended = jnp.where(hit[:, None, None], global_out[global_slot][None], attended)
    attention_out = attended.reshape(tok_here, width_here)
    share = lax.psum_scatter(
        lax.dot_general(
            out_weight, attention_out, (((0,), (1,)), ((), ())), preferred_element_type=jnp.float32
        ).astype(jnp.bfloat16),
        "head",
        scatter_dimension=0,
        tiled=True,
    ).astype(jnp.float32)
    return share.T.astype(jnp.bfloat16)


def solution(mesh):
    in_specs = (
        P("seq", "head"),
        P("seq", "head"),
        P("seq", "head"),
        P("head", None),
        P(),
        P(),
        P("head"),
        P(),
        P(),
    )
    out_specs = P("seq", "head")
    return jax.shard_map(
        on_device, mesh=mesh, in_specs=in_specs, out_specs=out_specs, check_vma=False
    )
```

profile of v0, /device:TPU:0, one launch (start us, length us, event | category | flops | bytes accessed | tf_op | source)
XLA Modules:
  0.0 288.8 jit_solution(7155592734332625758)
XLA Ops:
  8.0 1.2 copy.100
  9.3 1.2 copy.101
  10.6 1.1 convert.4
  11.7 0.2 copy.109
  11.9 0.3 fusion.42
  12.2 1.5 multiply_subtract_fusion
  13.8 1.2 fusion.33
  15.0 3.1 %collective-permute-start = (bf16[2,128,1024]{1,2,0:T(8,128)(2,1)}, bf16[2,128,1024]{1,2,0:T(8,128)(2,1)}, u32[]{:S(2)}, u32[]{:S(2)}) collective-permute-start(bf16[2,128,1024]{1,2,0:T(8,128)(2,1)} %get-tuple-element.13), channel_id=1, source_target_pairs={{0,4},{4,8},{8,12},{12,16},{16,20},{20,24},{24,28},{1,5},{5,9},{9,... | collective-permute-start | bytes 1572872 | tf_op jit(solution)/shard_map/ppermute | solution.py:23
  18.1 1.3 collective-permute-start.1
  19.4 0.4 reshape.472
  20.0 1.3 copy.130
  21.5 0.3 convert_reduce_fusion
  21.9 0.2 select_reduce_fusion
  22.3 0.4 reshape.471
  22.7 1.4 copy.129
  24.0 1.6 gather_fusion.1
  25.7 1.6 gather_fusion
  27.3 0.6 gather_fusion.2
  27.8 1.1 select_convert_fusion
  29.0 0.4 reshape.473
  29.4 1.3 copy.133
  30.7 1.1 pad_maximum_fusion.1
  31.9 2.8 gather_fusion.3
  34.7 6.4 %all-to-all-start = ((bf16[2,8,2,64,1024]{4,3,0,2,1:T(8,128)(2,1)}), bf16[2,8,2,64,1024]{4,3,0,2,1:T(8,128)(2,1)}, u32[]{:S(2)}, u32[]{:S(2)}) async-start(bf16[2,8,2,64,1024]{4,3,0,2,1:T(8,128)(2,1)} %bitcast.165), calls=%async_computation | async-start | bytes 8388608 | tf_op jit(solution)/shard_map/all_to_all | solution.py:139
  41.2 0.7 fusion.63
  41.8 0.7 fusion.62
  42.7 1.4 reshape.474
  44.1 0.1 broadcast_in_dim.164
  44.2 0.1 broadcast_in_dim.165
  44.3 0.9 copy.137
  45.2 1.3 compare_and_fusion.1
  46.7 1.2 compare_and_fusion
  48.1 0.2 dynamic-slice_reduce_fusion
  48.3 64.6 %all-reduce.4.cloned.1.call-done = bf16[3,2,64,1024]{3,2,1,0:T(8,128)(2,1)} async-done(((bf16[3,2,64,1024]{3,2,1,0:T(8,128)(2,1)}), bf16[3,2,64,1024]{3,2,1,0:T(8,128)(2,1)}) %all-reduce.4.cloned.1.call-update) | async-done | bytes 786448 | tf_op jit(solution)/shard_map/psum | solution.py:122
  112.9 1.0 slice.100
  114.0 0.3 fusion.64
  114.3 0.2 bitcast_reduce_fusion
  114.5 12.1 %pmax.7 = f32[2,8,64]{2,0,1:T(2,128)S(1)} all-reduce(f32[2,8,64]{2,0,1:T(2,128)S(1)} %bitcast_reduce_fusion), channel_id=1, replica_groups=mesh['seq'=8,'head'=4] {'seq'}, use_global_device_ids=true, to_apply=%region_2.3 | all-reduce | flops 1024 | bytes 8192 | tf_op jit(solution)/shard_map/pmax | solution.py:163
  126.7 0.5 fusion.30
  127.1 11.8 %psum.23 = bf16[2,64,8]{1,0,2:T(2,128)(2,1)S(1)} all-reduce(bf16[2,64,8]{1,0,2:T(2,128)(2,1)S(1)} %bitcast.194), channel_id=1, replica_groups=mesh['seq'=8,'head'=4] {'seq'}, use_global_device_ids=true, to_apply=%region_5.6 | all-reduce | flops 1024 | bytes 4096 | tf_op jit(solution)/shard_map/psum | solution.py:171
  139.0 2.1 fusion.18
  141.1 0.2 reduce-scatter.2.cloned.1.call-start
  141.4 2.8 pad_maximum_fusion
  144.1 3.0 %copy.110 = bf16[2,512,1024]{2,1,0:T(8,128)(2,1)S(1)} copy(bf16[2,512,1024]{1,2,0:T(8,128)(2,1)} %pad_maximum_fusion) | data formatting | bytes 4194304 | tf_op jit(solution)/shard_map/concatenate | solution.py:21
  147.1 46.8 %all-reduce.6.cloned.1.call-done = bf16[2,64,8,128]{3,1,0,2:T(8,128)(2,1)} async-done(((bf16[2,64,8,128]{3,1,0,2:T(8,128)(2,1)}), bf16[2,64,8,128]{3,1,0,2:T(8,128)(2,1)}) %all-reduce.6.cloned.1.call-update) | async-done | bytes 262160 | tf_op jit(solution)/shard_map/psum | solution.py:170
  194.0 1.2 divide_convert_fusion.1
  195.4 1.2 fusion.23
  196.6 1.1 fusion.22
  197.6 1.2 fusion.21
  198.8 1.1 fusion.20
  200.0 1.1 fusion.19
  201.1 1.6 broadcast_dynamic-update-slice_fusion
  202.7 4.6 %gather_fusion.4 = bf16[12,2,64,1024]{3,2,1,0:T(8,128)(2,1)} fusion(bf16[2,8,2,64,1024]{4,3,0,2,1:T(8,128)(2,1)} %all-to-all-done, s32[12]{0:T(128)S(1)} %fusion.55), kind=kCustom, calls=%fused_computation.4 | custom fusion | bytes 6291552 | tf_op jit(solution)/shard_map/gather | solution.py:142
  207.3 2.4 copy.116
  209.7 2.2 constant_dynamic-update-slice_fusion
  211.9 10.2 %fusion.60 = (bf16[1,4,10,64,1024]{4,3,2,1,0:T(8,128)(2,1)}, bf16[1,4,10,64,1024]{4,3,2,1,0:T(8,128)(2,1)}) fusion(bf16[2,4,10,64,1024]{4,3,2,1,0:T(8,128)(2,1)} %constant_dynamic-update-slice_fusion), kind=kLoop, calls=%fused_computation.121 | loop fusion | bytes 20971520 | tf_op jit(solution)/shard_map/slice | solution.py:155
  222.1 4.0 %copy.140 = bf16[320,8,8,128]{3,2,1,0:T(8,128)(2,1)S(1)} copy(bf16[320,8,8,128]{3,1,2,0:T(8,128)(2,1)} %bitcast.160) | data formatting | bytes 10485760
  226.1 1.4 copy.141
  227.5 2.5 fusion.5
  230.0 1.6 fusion.6
  231.7 2.8 divide_convert_fusion
  234.5 0.3 copy.126
  235.0 3.8 %fusion.4 = bf16[4096,256]{0,1:T(8,128)(2,1)} fusion(bf16[1024,4096]{1,0:T(8,128)(2,1)S(1)} %bitcast.196, bf16[256,1024]{1,0:T(8,128)(2,1)S(1)} %bitcast.185, bf16[256,1024]{1,0:T(8,128)(2,1)S(1)} %bitcast.186, bf16[32,8,8,128]{3,2,1,0:T(8,128)(2,1)S(1)} %bitcast.190, pred[256]{0:T(512)(128)(4,1)S(1)} %broadcast_in_dim.151, ...), kind=kOutput, calls=%fused_computation.12 | convolution fusion | flops 2149056512 | bytes 12059136 | tf_op jit(solution)/shard_map/dot_general | solution.py:184
  238.8 43.4 %reduce-scatter.2.cloned.1.call-done = bf16[1024,256]{0,1:T(8,128)(2,1)} async-done(((bf16[4096,256]{0,1:T(8,128)(2,1)}), bf16[1024,256]{0,1:T(8,128)(2,1)}) %reduce-scatter.2.cloned.1.call-update) | async-done | bytes 524304 | tf_op jit(solution)/shard_map/reduce_scatter | solution.py:183
  (66 shorter events, 1.9 us)
Async XLA Ops:
  6.5 5.1 %copy-start.1 = (bf16[256,1024]{1,0:T(8,128)(2,1)S(1)}, bf16[256,1024]{1,0:T(8,128)(2,1)}, u32[]{:S(2)}) copy-start(bf16[256,1024]{1,0:T(8,128)(2,1)} %param.11) | copy-start | bytes 1572868
  6.5 106.4 %all-reduce.4.cloned.1.call-start = ((), (), s32[]{:S(2)}) async-start(), calls=%async_computation.2 | async-start | bytes 1572864 | tf_op jit(solution)/shard_map/psum | solution.py:122
  11.7 8.2 %copy-start.3 = (s32[32,3]{0,1:T(4,128)S(1)}, s32[32,3]{0,1:T(4,128)}, u32[]{:S(2)}) copy-start(s32[32,3]{0,1:T(4,128)} %param.14) | copy-start | bytes 1156
  12.2 10.0 %copy-start.4 = (s32[2]{0:T(128)S(1)}, s32[2]{0:T(128)}, u32[]{:S(2)}) copy-start(s32[2]{0:T(128)} %param.13) | copy-start | bytes 28
  15.0 126.4 %collective-permute-start = (bf16[2,128,1024]{1,2,0:T(8,128)(2,1)}, bf16[2,128,1024]{1,2,0:T(8,128)(2,1)}, u32[]{:S(2)}, u32[]{:S(2)}) collective-permute-start(bf16[2,128,1024]{1,2,0:T(8,128)(2,1)} %get-tuple-element.13), channel_id=1, source_target_pairs={{0,4},{4,8},{8,12},{12,16},{16,20},{20,24},{24,28},{1,5},{5,9},{9,... | collective-permute-start | bytes 1572872 | tf_op jit(solution)/shard_map/ppermute | solution.py:23
  18.1 123.2 %collective-permute-start.1 = (bf16[2,128,1024]{1,2,0:T(8,128)(2,1)}, bf16[2,128,1024]{1,2,0:T(8,128)(2,1)}, u32[]{:S(2)}, u32[]{:S(2)}) collective-permute-start(bf16[2,128,1024]{1,2,0:T(8,128)(2,1)} %get-tuple-element.14), channel_id=1, source_target_pairs={{4,0},{8,4},{12,8},{16,12},{20,16},{24,20},{28,24},{5,1},{9,5},{13... | collective-permute-start | bytes 1572872 | tf_op jit(solution)/shard_map/ppermute | solution.py:25
  34.7 7.9 %copy-start.5 = (s32[8]{0:T(128)S(1)}, s32[8]{0:T(128)}, u32[]{:S(2)}) copy-start(s32[8]{0:T(128)} %param.15) | copy-start | bytes 100
  34.7 168.0 %all-to-all-start = ((bf16[2,8,2,64,1024]{4,3,0,2,1:T(8,128)(2,1)}), bf16[2,8,2,64,1024]{4,3,0,2,1:T(8,128)(2,1)}, u32[]{:S(2)}, u32[]{:S(2)}) async-start(bf16[2,8,2,64,1024]{4,3,0,2,1:T(8,128)(2,1)} %bitcast.165), calls=%async_computation | async-start | bytes 8388608 | tf_op jit(solution)/shard_map/all_to_all | solution.py:139
  41.1 152.9 %all-reduce.6.cloned.1.call-start = ((), (), s32[]{:S(2)}) async-start(), calls=%async_computation.3 | async-start | bytes 524288 | tf_op jit(solution)/shard_map/psum | solution.py:170
  141.1 141.1 %reduce-scatter.2.cloned.1.call-start = ((), (), s32[]{:S(2)}) async-start(), calls=%async_computation.4 | async-start | bytes 2621440 | tf_op jit(solution)/shard_map/reduce_scatter | solution.py:183
  195.4 5.7 %slice-start = ((bf16[3,2,64,1024]{3,2,1,0:T(8,128)(2,1)}), bf16[2,2,64,1024]{3,2,1,0:T(8,128)(2,1)S(1)}, s32[]{:S(2)}) async-start(bf16[3,2,64,1024]{3,2,1,0:T(8,128)(2,1)} %all-reduce.4.cloned.1.call-done), calls=%async_computation.5 | async-start | bytes 1048576 | tf_op jit(solution)/shard_map/slice | solution.py:148
  222.1 4.1 %copy-start = (bf16[1,4,10,64,1024]{4,3,2,1,0:T(8,128)(2,1)S(1)}, bf16[1,4,10,64,1024]{4,3,2,1,0:T(8,128)(2,1)}, u32[]{:S(2)}) copy-start(bf16[1,4,10,64,1024]{4,3,2,1,0:T(8,128)(2,1)} %get-tuple-element.8) | copy-start | bytes 15728644
  226.1 1.4 copy-start.2
  230.0 4.9 %slice-start.1 = ((s8[8388608]{0:T(1024)(128)(4,1)}), s8[4194304]{0:T(1024)(128)(4,1)S(1)}, s32[]{:S(2)}) async-start(s8[8388608]{0:T(1024)(128)(4,1)} %bitcast.195), calls=%async_computation.6 | async-start | bytes 8388608
  231.7 3.3 %slice-start.2 = ((s8[8388608]{0:T(1024)(128)(4,1)}), s8[4194304]{0:T(1024)(128)(4,1)S(1)}, s32[]{:S(2)}) async-start(s8[8388608]{0:T(1024)(128)(4,1)} %bitcast.195), calls=%async_computation.7 | async-start | bytes 8388608
Sparse Core Ops, SparseCore 0:
  29.1 83.7 all-reduce.3
  141.2 52.6 all-reduce.5
  239.0 43.2 reduce-scatter.1
where the time goes:
time: 290 us; the launch traced here: 289 us
  waiting for transfers between devices  155 us (53%)
  local copies, waits for them, and re-layouts  56.2 us (19%)
  blocking collectives  23.9 us (8%)
  other arithmetic  16.1 us (6%)
  between operations  15 us (5%)
  matrix products  11.5 us (4%)
  starting transfers between devices  11.1 us (4%)
    psum x1, waiting for transfers between devices, on_device(): shared = lax.psum(masked.astype(jnp.bfloat16), 'seq')  64.6 us
    psum x1, waiting for transfers between devices, on_device(): lax.psum(partial_mix.astype(jnp.bfloat16), 'seq').astype(jnp.float32)  46.8 us
    reduce_scatter x1, waiting for transfers between devices, on_device(): lax.psum_scatter(lax.dot_general(out_weight, attention_out, (((0,), (1,))...  43.4 us
    unnamed x32, local copies, waits for them, and re-layouts  16.5 us
    pmax x1, blocking collectives, on_device(): peak = lax.pmax(local_peak, 'seq')  12.1 us
    psum x1, blocking collectives, on_device(): lax.psum(partial_total.astype(jnp.bfloat16), 'seq').astype(jnp.float32)  11.8 us
    slice x1, local copies, waits for them, and re-layouts, on_device(): attended = block_attend(query_view, all_kv[0], all_kv[1], all_valid)  10.2 us
    gather x2, local copies, waits for them, and re-layouts, on_device(): incoming[:, my_owners, my_ranks]  6.98 us
  transfers between devices with their start and end apart: 6, of which 3 were waited for; matrix products, arithmetic and copies ran while one was open for 14% of the time, Pallas kernels for 0%

commit v1 on v0

--- a/solution.py
+++ b/solution.py
@@ -167,7 +167,9 @@
         "ghqk,khd->gqhd", expo.astype(jnp.bfloat16), value_grid, preferred_element_type=jnp.float32
     )
     mix_sum, total_sum = (
-        lax.psum(partial_mix.astype(jnp.bfloat16), "seq").astype(jnp.float32),
+        jnp.sum(lax.all_gather(partial_mix.astype(jnp.bfloat16), "seq"), axis=0).astype(
+            jnp.float32
+        ),
         lax.psum(partial_total.astype(jnp.bfloat16), "seq").astype(jnp.float32),
     )
     global_out = (

time: 290 us -> 247 us (0.85)
  waiting for transfers between devices: 155 us -> 108 us
  matrix products: 11.5 us -> 14.9 us
    psum x1 -> x0, waiting for transfers between devices: 46.8 us -> none  [on_device(): lax.psum(partial_mix.astype(jnp.bfloat16), 'seq').astype(jnp.float32)]
    dot_general x1, matrix products: 3.83 us -> 7.17 us  [on_device(): lax.dot_general(out_weight, attention_out, (((0,), (1,)), ((), ())), pref...]
    unnamed x32 -> x28, local copies, waits for them, and re-layouts: 16.5 us -> 16.3 us
  transfers between devices with their start and end apart: 6 -> 6, of which waited for: 3 -> 2; matrix products, arithmetic and copies ran while one was open for 14% -> 29% of each run, Pallas kernels for 0% -> 0%
where the time goes in v1:
time: 247 us; the launch traced here: 246 us
  waiting for transfers between devices  108 us (44%)
  local copies, waits for them, and re-layouts  56.1 us (23%)
  blocking collectives  23.9 us (10%)
  other arithmetic  17.1 us (7%)
  matrix products  14.9 us (6%)
  between operations  14.9 us (6%)
  starting transfers between devices  11.1 us (4%)
    psum x1, waiting for transfers between devices, on_device(): shared = lax.psum(masked.astype(jnp.bfloat16), 'seq')  64.8 us
    reduce_scatter x1, waiting for transfers between devices, on_device(): lax.psum_scatter(lax.dot_general(out_weight, attention_out, (((0,), (1,))...  43.6 us
    unnamed x28, local copies, waits for them, and re-layouts  16.3 us
    pmax x1, blocking collectives, on_device(): peak = lax.pmax(local_peak, 'seq')  12.1 us
    psum x1, blocking collectives, on_device(): lax.psum(partial_total.astype(jnp.bfloat16), 'seq').astype(jnp.float32)  11.8 us
    slice x1, local copies, waits for them, and re-layouts, on_device(): attended = block_attend(query_view, all_kv[0], all_kv[1], all_valid)  10.3 us
    dot_general x1, matrix products, on_device(): lax.dot_general(out_weight, attention_out, (((0,), (1,)), ((), ())), pref...  7.17 us
    gather x2, local copies, waits for them, and re-layouts, on_device(): incoming[:, my_owners, my_ranks]  6.98 us
  transfers between devices with their start and end apart: 6, of which 2 were waited for; matrix products, arithmetic and copies ran while one was open for 29% of the time, Pallas kernels for 0%

profile of v1, /device:TPU:0, one launch (start us, length us, event | category | flops | bytes accessed | tf_op | source)
XLA Modules:
  0.0 246.5 jit_solution(12216072000394120666)
XLA Ops:
  8.0 1.2 copy.144
  9.3 1.2 copy.145
  10.6 1.1 convert.5
  11.7 0.2 copy.153
  11.9 0.3 fusion.42
  12.2 1.5 multiply_subtract_fusion
  13.8 1.2 fusion.33
  15.0 3.2 %collective-permute-start = (bf16[2,128,1024]{1,2,0:T(8,128)(2,1)}, bf16[2,128,1024]{1,2,0:T(8,128)(2,1)}, u32[]{:S(2)}, u32[]{:S(2)}) collective-permute-start(bf16[2,128,1024]{1,2,0:T(8,128)(2,1)} %get-tuple-element.13), channel_id=1, source_target_pairs={{0,4},{4,8},{8,12},{12,16},{16,20},{20,24},{24,28},{1,5},{5,9},{9,... | collective-permute-start | bytes 1572872 | tf_op jit(solution)/shard_map/ppermute | solution.py:23
  18.2 1.3 collective-permute-start.1
  19.4 0.4 reshape.477
  20.1 1.3 copy.174
  21.5 0.3 convert_reduce_fusion
  21.9 0.2 select_reduce_fusion
  22.3 0.4 reshape.476
  22.7 1.4 copy.173
  24.1 1.6 gather_fusion.1
  25.7 1.6 gather_fusion
  27.3 0.6 gather_fusion.2
  27.9 1.2 select_convert_fusion
  29.1 0.4 reshape.478
  29.5 1.3 copy.177
  30.8 1.1 pad_maximum_fusion.1
  32.0 2.8 %gather_fusion.3 = bf16[16,2,64,1024]{3,2,1,0:T(8,128)(2,1)} fusion(bf16[2,4,64,1024]{3,2,1,0:T(8,128)(2,1)S(1)} %pad_maximum_fusion.1, s32[1024]{0:T(1024)S(1)} %get-tuple-element.29), kind=kCustom, calls=%fused_computation.3 | custom fusion | bytes 8388672 | tf_op jit(solution)/shard_map/gather | solution.py:138
  34.8 6.4 %all-to-all-start = ((bf16[2,8,2,64,1024]{4,3,0,2,1:T(8,128)(2,1)}), bf16[2,8,2,64,1024]{4,3,0,2,1:T(8,128)(2,1)}, u32[]{:S(2)}, u32[]{:S(2)}) async-start(bf16[2,8,2,64,1024]{4,3,0,2,1:T(8,128)(2,1)} %bitcast.166), calls=%async_computation | async-start | bytes 8388608 | tf_op jit(solution)/shard_map/all_to_all | solution.py:139
  41.2 1.4 reshape.479
  42.8 0.1 broadcast_in_dim.164
  43.0 0.1 broadcast_in_dim.165
  43.1 0.9 copy.181
  44.0 0.6 fusion.62
  44.6 0.6 fusion.63
  45.2 1.2 compare_and_fusion.1
  46.6 1.2 compare_and_fusion
  48.1 0.2 dynamic-slice_reduce_fusion
  48.3 64.8 %all-reduce.3.cloned.1.call-done = bf16[3,2,64,1024]{3,2,1,0:T(8,128)(2,1)} async-done(((bf16[3,2,64,1024]{3,2,1,0:T(8,128)(2,1)}), bf16[3,2,64,1024]{3,2,1,0:T(8,128)(2,1)}) %all-reduce.3.cloned.1.call-update) | async-done | bytes 786448 | tf_op jit(solution)/shard_map/psum | solution.py:122
  113.0 1.0 slice.100
  114.1 0.3 fusion.64
  114.4 0.2 bitcast_reduce_fusion
  114.6 12.1 %pmax.7 = f32[2,8,64]{2,0,1:T(2,128)S(1)} all-reduce(f32[2,8,64]{2,0,1:T(2,128)S(1)} %bitcast_reduce_fusion), channel_id=1, replica_groups=mesh['seq'=8,'head'=4] {'seq'}, use_global_device_ids=true, to_apply=%region_2.3 | all-reduce | flops 1024 | bytes 8192 | tf_op jit(solution)/shard_map/pmax | solution.py:163
  126.8 0.5 fusion.30
  127.2 11.8 %psum.15 = bf16[2,64,8]{1,0,2:T(2,128)(2,1)S(1)} all-reduce(bf16[2,64,8]{1,0,2:T(2,128)(2,1)S(1)} %bitcast.196), channel_id=1, replica_groups=mesh['seq'=8,'head'=4] {'seq'}, use_global_device_ids=true, to_apply=%region_5.6 | all-reduce | flops 1024 | bytes 4096 | tf_op jit(solution)/shard_map/psum | solution.py:173
  139.1 2.1 fusion.18
  141.2 0.2 reduce-scatter.2.cloned.1.call-start
  141.5 2.7 %pad_maximum_fusion = bf16[2,512,1024]{1,2,0:T(8,128)(2,1)} fusion(bf16[2,128,1024]{1,2,0:T(8,128)(2,1)} %collective-permute-done.1, bf16[1,256,1024]{1,2,0:T(8,128)(2,1)S(1)} %bitcast.177, bf16[1,256,1024]{1,2,0:T(8,128)(2,1)S(1)} %bitcast.165, bf16[2,128,1024]{1,2,0:T(8,128)(2,1)} %collective-permute-done), kind=kLoop, calls=%fused_computation.20 | loop fusion | flops 8388608 | bytes 4194304 | tf_op jit(solution)/shard_map/concatenate | solution.py:21
  144.2 3.0 %copy.154 = bf16[2,512,1024]{2,1,0:T(8,128)(2,1)S(1)} copy(bf16[2,512,1024]{1,2,0:T(8,128)(2,1)} %pad_maximum_fusion) | data formatting | bytes 4194304 | tf_op jit(solution)/shard_map/concatenate | solution.py:21
  147.2 1.1 fusion.23
  148.3 1.1 fusion.22
  149.4 1.1 fusion.21
  150.5 1.1 fusion.20
  151.7 1.1 fusion.19
  152.8 1.6 broadcast_dynamic-update-slice_fusion
  154.4 4.6 %gather_fusion.4 = bf16[12,2,64,1024]{3,2,1,0:T(8,128)(2,1)} fusion(bf16[2,8,2,64,1024]{4,3,0,2,1:T(8,128)(2,1)} %all-to-all-done, s32[12]{0:T(128)S(1)} %fusion.55), kind=kCustom, calls=%fused_computation.4 | custom fusion | bytes 6291552 | tf_op jit(solution)/shard_map/gather | solution.py:142
  159.0 2.4 copy.160
  161.4 2.2 constant_dynamic-update-slice_fusion
  163.5 10.3 %fusion.60 = (bf16[1,4,10,64,1024]{4,3,2,1,0:T(8,128)(2,1)}, bf16[1,4,10,64,1024]{4,3,2,1,0:T(8,128)(2,1)}) fusion(bf16[2,4,10,64,1024]{4,3,2,1,0:T(8,128)(2,1)} %constant_dynamic-update-slice_fusion), kind=kLoop, calls=%fused_computation.121 | loop fusion | bytes 20971520 | tf_op jit(solution)/shard_map/slice | solution.py:155
  173.8 4.0 %copy.184 = bf16[320,8,8,128]{3,2,1,0:T(8,128)(2,1)S(1)} copy(bf16[320,8,8,128]{3,1,2,0:T(8,128)(2,1)} %bitcast.161) | data formatting | bytes 10485760
  177.9 1.4 copy.185
  179.3 2.5 %fusion.5 = (f32[4,8,64]{2,1,0:T(8,128)S(1)}, f32[4,8,64,640]{3,2,1,0:T(8,128)S(1)}) fusion(pred[4,8,640]{2,1,0:T(8,128)(4,1)S(1)} %broadcast_in_dim.165, bf16[4,640,8,128]{3,2,1,0:T(8,128)(2,1)S(1)} %bitcast.162, bf16[4,64,8,128]{1,0,3,2:T(4,128)(2,1)S(1)} %copy-done.2), kind=kOutput, calls=%fused_computation.13 | convolution fusion | flops 339474432 | bytes 11038720 | tf_op jit(solution)/shard_map/bqhd,bshd->bhqs/dot_general | solution.py:71
  181.8 1.6 fusion.6
  183.4 2.8 %divide_convert_fusion = bf16[4,64,8,128]{3,1,2,0:T(8,128)(2,1)S(1)} fusion(bf16[4,640,8,128]{3,2,1,0:T(8,128)(2,1)S(1)} %bitcast.175, f32[4,8,64,640]{3,2,1,0:T(8,128)S(1)} %get-tuple-element.28, f32[4,8,64]{2,1,0:T(8,128)S(1)} %get-tuple-element.27, pred[4,8,640]{2,1,0:T(8,128)(4,1)S(1)} %broadcast_in_dim.165, f32[4,64,8]{1,2,0:T(8,128)S(1)} %bitcast.195), kind=kOutput, calls=%fused_computation.44 | convolution fusion | flops 341311488 | bytes 11046912 | tf_op jit(solution)/shard_map/bhqs,bshd->bqhd/dot_general | solution.py:80
  186.2 0.3 copy.170
  186.6 2.0 reduce_sum.50
  188.6 0.2 divide_convert_fusion.1
  189.2 7.2 %fusion.4 = bf16[4096,256]{0,1:T(8,128)(2,1)} fusion(bf16[1024,4096]{1,0:T(8,128)(2,1)} %param.12, bf16[256,1024]{1,0:T(8,128)(2,1)S(1)} %bitcast.187, bf16[256,1024]{1,0:T(8,128)(2,1)S(1)} %bitcast.188, bf16[32,8,8,128]{3,2,1,0:T(8,128)(2,1)S(1)} %bitcast.192, pred[256]{0:T(512)(128)(4,1)S(1)} %broadcast_in_dim.151, pred[256]{0:T(512)(128)(4,1)S(1)} %broadcast_in_dim.142), kind=kOutput, calls=%fused_computation.12 | convolution fusion | flops 2149056512 | bytes 12059136 | tf_op jit(solution)/shard_map/dot_general | solution.py:186
  196.4 43.6 %reduce-scatter.2.cloned.1.call-done = bf16[1024,256]{0,1:T(8,128)(2,1)} async-done(((bf16[4096,256]{0,1:T(8,128)(2,1)}), bf16[1024,256]{0,1:T(8,128)(2,1)}) %reduce-scatter.2.cloned.1.call-update) | async-done | bytes 524304 | tf_op jit(solution)/shard_map/reduce_scatter | solution.py:185
  (62 shorter events, 1.9 us)
Async XLA Ops:
  6.5 5.1 %copy-start.1 = (bf16[256,1024]{1,0:T(8,128)(2,1)S(1)}, bf16[256,1024]{1,0:T(8,128)(2,1)}, u32[]{:S(2)}) copy-start(bf16[256,1024]{1,0:T(8,128)(2,1)} %param.11) | copy-start | bytes 1572868
  6.5 106.5 %all-reduce.3.cloned.1.call-start = ((), (), s32[]{:S(2)}) async-start(), calls=%async_computation.2 | async-start | bytes 1572864 | tf_op jit(solution)/shard_map/psum | solution.py:122
  11.7 8.2 %copy-start.3 = (s32[32,3]{0,1:T(4,128)S(1)}, s32[32,3]{0,1:T(4,128)}, u32[]{:S(2)}) copy-start(s32[32,3]{0,1:T(4,128)} %param.14) | copy-start | bytes 1156
  12.2 10.0 %copy-start.4 = (s32[2]{0:T(128)S(1)}, s32[2]{0:T(128)}, u32[]{:S(2)}) copy-start(s32[2]{0:T(128)} %param.13) | copy-start | bytes 28
  15.0 126.5 %collective-permute-start = (bf16[2,128,1024]{1,2,0:T(8,128)(2,1)}, bf16[2,128,1024]{1,2,0:T(8,128)(2,1)}, u32[]{:S(2)}, u32[]{:S(2)}) collective-permute-start(bf16[2,128,1024]{1,2,0:T(8,128)(2,1)} %get-tuple-element.13), channel_id=1, source_target_pairs={{0,4},{4,8},{8,12},{12,16},{16,20},{20,24},{24,28},{1,5},{5,9},{9,... | collective-permute-start | bytes 1572872 | tf_op jit(solution)/shard_map/ppermute | solution.py:23
  18.2 123.3 %collective-permute-start.1 = (bf16[2,128,1024]{1,2,0:T(8,128)(2,1)}, bf16[2,128,1024]{1,2,0:T(8,128)(2,1)}, u32[]{:S(2)}, u32[]{:S(2)}) collective-permute-start(bf16[2,128,1024]{1,2,0:T(8,128)(2,1)} %get-tuple-element.14), channel_id=1, source_target_pairs={{4,0},{8,4},{12,8},{16,12},{20,16},{24,20},{28,24},{5,1},{9,5},{13... | collective-permute-start | bytes 1572872 | tf_op jit(solution)/shard_map/ppermute | solution.py:25
  34.7 8.0 %copy-start.5 = (s32[8]{0:T(128)S(1)}, s32[8]{0:T(128)}, u32[]{:S(2)}) copy-start(s32[8]{0:T(128)} %param.15) | copy-start | bytes 100
  34.8 119.6 %all-to-all-start = ((bf16[2,8,2,64,1024]{4,3,0,2,1:T(8,128)(2,1)}), bf16[2,8,2,64,1024]{4,3,0,2,1:T(8,128)(2,1)}, u32[]{:S(2)}, u32[]{:S(2)}) async-start(bf16[2,8,2,64,1024]{4,3,0,2,1:T(8,128)(2,1)} %bitcast.166), calls=%async_computation | async-start | bytes 8388608 | tf_op jit(solution)/shard_map/all_to_all | solution.py:139
  41.2 145.4 %all-gather.3.cloned.1.call-start = ((), (), s32[]{:S(2)}) async-start(), calls=%async_computation.4 | async-start | bytes 2359296 | tf_op jit(solution)/shard_map/all_gather | solution.py:170
  141.2 98.7 %reduce-scatter.2.cloned.1.call-start = ((), (), s32[]{:S(2)}) async-start(), calls=%async_computation.3 | async-start | bytes 2621440 | tf_op jit(solution)/shard_map/reduce_scatter | solution.py:185
  147.2 5.5 %slice-start = ((bf16[3,2,64,1024]{3,2,1,0:T(8,128)(2,1)}), bf16[2,2,64,1024]{3,2,1,0:T(8,128)(2,1)S(1)}, s32[]{:S(2)}) async-start(bf16[3,2,64,1024]{3,2,1,0:T(8,128)(2,1)} %all-reduce.3.cloned.1.call-done), calls=%async_computation.5 | async-start | bytes 1048576 | tf_op jit(solution)/shard_map/slice | solution.py:148
  173.8 4.1 %copy-start = (bf16[1,4,10,64,1024]{4,3,2,1,0:T(8,128)(2,1)S(1)}, bf16[1,4,10,64,1024]{4,3,2,1,0:T(8,128)(2,1)}, u32[]{:S(2)}) copy-start(bf16[1,4,10,64,1024]{4,3,2,1,0:T(8,128)(2,1)} %get-tuple-element.8) | copy-start | bytes 15728644
  177.9 1.4 copy-start.2
Sparse Core Ops, SparseCore 0:
  29.2 83.8 all-reduce.2
  141.4 27.0 all-gather.2
  196.5 43.3 reduce-scatter.1
